TPU v7x, 128 devices: a whole 4x4x4 slice. The times are simulated.
128 devices in a mesh: tm: 64 (over x, y_hi, z, core), mp: 2 (over y_lo).
Axes of the slice: x: 4, y: 4 (y_hi: 2, y_lo: 2; y = y_hi * 2 + y_lo), z: 4, core: 2. Of those that a mesh axis runs over, the one named last changes fastest.
Arguments:
- frames: bfloat16 [32768, 1024], P('tm'), may hold values from -24 to 24
- cotangent: bfloat16 [32768, 1024], P('tm'), may hold values from -20 to 20
- weights: bfloat16 [1024, 4, 1024], P(None, None, 'mp'), may hold values from -4 to 4
- summary: bfloat16 [64, 1024], replicated, may hold values from -5 to 5
- owners: int32 [64], replicated, may hold values from 0 to 63, as said below
Outputs:
- grad_frames: bfloat16 [32768, 1024], P(('tm', 'mp'))
- grad_weights: float32 [1024, 4, 1024], P('tm', None, 'mp')
- grad_summary: float32 [64, 1024], replicated
Inputs may be any that keep to these rules, and one draw needn't show every extreme that they name: owners[g] is the index of the block of 512 frames that global token g summarizes.
All inputs are finite; a program needn't handle non-finite values.
Results may differ from a plain program's by a relative error of at most 0.04.
Values may be sent and summed in bfloat16 or wider, within the bound.
No kernel may reach another device: no remote copies, remote signals or barrier semaphores. Data moves between devices by JAX's collectives and lax.ppermute only.
A program may use at most 128 MiB of HBM per device.

v0:
```python
import jax
import jax.numpy as jnp
from jax import lax
from jax.sharding import PartitionSpec as P

HEAD_DIM = 64
WINDOW = 512


EPSILON = 1e-05
PRECISE = lax.Precision.HIGHEST


def from_behind(shard, axis, by):
    devices = lax.axis_size(axis)
    pairs = [(i, i + by) for i in range(devices) if 0 <= i + by < devices]
    return lax.ppermute(shard, axis, pairs)


def normalize(rows_in):
    inverse = lax.rsqrt(jnp.mean(rows_in * rows_in, axis=-1, keepdims=True) + EPSILON)
    return (rows_in * inverse, inverse)


def norm_back(gradient, unit_rows, inverse):
    return (gradient - unit_rows * jnp.mean(gradient * unit_rows, axis=-1, keepdims=True)) * inverse


def product(form, left, right):
    return jnp.einsum(form, left, right, preferred_element_type=jnp.float32)


def window_mask(row_count, lead, root):
    query_pos = lax.broadcasted_iota(jnp.int32, (row_count, row_count + lead), 0)
    key_pos = lax.broadcasted_iota(jnp.int32, (row_count, row_count + lead), 1)
    inside = (key_pos > query_pos) & (key_pos <= query_pos + lead)
    return inside & (root - lead + key_pos >= 0)


def block_pass(queries, keys_ext, values_ext, keys_glob, values_glob, grad_rows, allowed):
    scaling = HEAD_DIM ** (-0.5)
    near_scores = product("qhe,khe->hqk", queries, keys_ext) * scaling
    far_scores = product("qhe,khe->hqk", queries, keys_glob) * scaling
    near_scores = jnp.where(allowed[None, :, :], near_scores, -jnp.inf)
    row_top = jnp.maximum(
        jnp.max(near_scores, axis=-1, keepdims=True), jnp.max(far_scores, axis=-1, keepdims=True)
    )
    near_exp = jnp.exp(near_scores - row_top)
    far_exp = jnp.exp(far_scores - row_top)
    row_total = jnp.sum(near_exp, axis=-1, keepdims=True) + jnp.sum(far_exp, axis=-1, keepdims=True)
    near_prob = (near_exp / row_total).astype(jnp.bfloat16)
    far_prob = (far_exp / row_total).astype(jnp.bfloat16)
    attended = (
        product("hqk,khe->qhe", near_prob, values_ext)
        + product("hqk,khe->qhe", far_prob, values_glob)
    ).astype(jnp.bfloat16)
    near_dot = product("qhe,khe->hqk", grad_rows, values_ext)
    far_dot = product("qhe,khe->hqk", grad_rows, values_glob)
    near_p32 = near_prob.astype(jnp.float32)
    far_p32 = far_prob.astype(jnp.float32)
    row_delta = jnp.sum(near_p32 * near_dot, axis=-1, keepdims=True) + jnp.sum(
        far_p32 * far_dot, axis=-1, keepdims=True
    )
    near_grad = (near_p32 * (near_dot - row_delta) * scaling).astype(jnp.bfloat16)
    far_grad = (far_p32 * (far_dot - row_delta) * scaling).astype(jnp.bfloat16)
    query_grad = (
        product("hqk,khe->qhe", near_grad, keys_ext) + product("hqk,khe->qhe", far_grad, keys_glob)
    ).astype(jnp.bfloat16)
    key_grad = product("hqk,qhe->khe", near_grad, queries)
    value_grad = product("hqk,qhe->khe", near_prob, grad_rows)
    glob_key_grad = product("hqk,qhe->khe", far_grad, queries)
    glob_value_grad = product("hqk,qhe->khe", far_prob, grad_rows)
    return (attended, query_grad, key_grad, value_grad, glob_key_grad, glob_value_grad)


def shards(frames, cotangent, weights, summary, owners):
    rows_here = frames.shape[0]
    width = frames.shape[1]
    local_width = weights.shape[2]
    heads_here = local_width // HEAD_DIM
    glob_count = summary.shape[0]
    shard_index = lax.axis_index("tm")
    shard_total = lax.axis_size("tm")
    frames32 = frames.astype(jnp.float32)
    unit_rows, inverse = normalize(frames32)
    normed = unit_rows.astype(jnp.bfloat16)
    block_mean = jnp.mean(frames32, axis=0, keepdims=True)
    pool_unit, pool_inv = normalize(block_mean)
    pooled = pool_unit.astype(jnp.bfloat16)
    owned_mask = (owners == shard_index).astype(jnp.float32)[:, None]
    kv_weights = weights[:, 1:3, :].reshape(width, 2 * local_width)
    anchor_own = (summary.astype(jnp.float32) + pooled.astype(jnp.float32)) * owned_mask
    own_unit, own_inv = normalize(anchor_own)
    kv_own = jnp.dot(own_unit.astype(jnp.bfloat16), kv_weights, preferred_element_type=jnp.float32)
    anchor, glob_kv32 = lax.psum((anchor_own, kv_own), "tm")
    glob_unit, glob_inv = normalize(anchor)
    glob_kv = glob_kv32.astype(jnp.bfloat16)
    glob_normed = glob_unit.astype(jnp.bfloat16)
    project = weights[:, :3, :].reshape(width, 3 * local_width)
    qkv = jnp.dot(normed, project, preferred_element_type=jnp.float32).astype(jnp.bfloat16)
    keys_local = qkv[:, local_width : 2 * local_width]
    values_local = qkv[:, 2 * local_width :]
    queries = qkv[:, :local_width].reshape(rows_here, heads_here, HEAD_DIM)
    grad_attended = jnp.dot(cotangent, weights[:, 3, :], preferred_element_type=jnp.float32).astype(
        jnp.bfloat16
    )
    grad_attended = grad_attended.reshape(rows_here, heads_here, HEAD_DIM)
    edge_keys, edge_values = from_behind((keys_local, values_local), "tm", 1)
    keys_ext = jnp.concatenate([edge_keys, keys_local], 0).reshape(
        rows_here + WINDOW, heads_here, HEAD_DIM
    )
    values_ext = jnp.concatenate([edge_values, values_local], 0).reshape(
        rows_here + WINDOW, heads_here, HEAD_DIM
    )
    keys_glob = glob_kv[:, :local_width].reshape(glob_count, heads_here, HEAD_DIM)
    values_glob = glob_kv[:, local_width:].reshape(glob_count, heads_here, HEAD_DIM)
    grad_kp = jnp.zeros((rows_here + WINDOW, heads_here, HEAD_DIM), jnp.float32)
    grad_vp = jnp.zeros((rows_here + WINDOW, heads_here, HEAD_DIM), jnp.float32)
    allowed = window_mask(WINDOW, WINDOW, shard_index * rows_here + 0)
    results = block_pass(
        queries, keys_ext, values_ext, keys_glob, values_glob, grad_attended, allowed
    )
    attended_parts = results[0]
    query_parts = results[1]
    grad_kp = grad_kp.at[0 : 2 * WINDOW].add(results[2])
    grad_vp = grad_vp.at[0 : 2 * WINDOW].add(results[3])
    grad_kg = results[4]
    grad_vg = results[5]
    attended = attended_parts.reshape(rows_here, local_width)
    grad_queries = query_parts.reshape(rows_here, local_width)
    back_keys, back_values = (
        from_behind(
            grad_kp[:WINDOW].reshape(WINDOW, local_width).astype(jnp.bfloat16), "tm", -1
        ).astype(jnp.float32),
        from_behind(
            grad_vp[:WINDOW].reshape(WINDOW, local_width).astype(jnp.bfloat16), "tm", -1
        ).astype(jnp.float32),
    )
    grad_keys = (
        grad_kp[WINDOW:]
        .reshape(rows_here, local_width)
        .at[rows_here - WINDOW :]
        .add(back_keys)
        .astype(jnp.bfloat16)
    )
    grad_values = (
        grad_vp[WINDOW:]
        .reshape(rows_here, local_width)
        .at[rows_here - WINDOW :]
        .add(back_values)
        .astype(jnp.bfloat16)
    )
    grad_cat = jnp.concatenate([grad_queries, grad_keys, grad_values], 1)
    glob_grads = jnp.concatenate(
        [grad_kg.reshape(glob_count, local_width), grad_vg.reshape(glob_count, local_width)], 1
    )
    kv_weights32 = kv_weights.astype(jnp.float32)
    glob_total = lax.psum(glob_grads, "tm")
    local_features = lax.dot_general(
        glob_total, kv_weights32, (((1,), (1,)), ((), ())), precision=PRECISE
    )
    summary_features = lax.psum(local_features.astype(jnp.bfloat16), "mp").astype(jnp.float32)
    grad_summary = norm_back(summary_features, glob_unit, glob_inv)
    pool_grads = lax.dot_general(
        owned_mask, grad_summary, (((0,), (0,)), ((), ())), precision=PRECISE
    )
    mean_grads = norm_back(pool_grads, pool_unit, pool_inv) / rows_here
    half_rows = rows_here // lax.axis_size("mp")
    start_row = lax.axis_index("mp") * half_rows
    feature_all = lax.dot_general(
        grad_cat, project, (((1,), (1,)), ((), ())), preferred_element_type=jnp.float32
    )
    feature_all = lax.psum(feature_all.astype(jnp.bfloat16), "mp").astype(jnp.float32)
    feature_grads = lax.dynamic_slice_in_dim(feature_all, start_row, half_rows, 0)
    my_unit = lax.dynamic_slice_in_dim(unit_rows, start_row, half_rows, 0)
    my_inverse = lax.dynamic_slice_in_dim(inverse, start_row, half_rows, 0)
    my_cotangent = lax.dynamic_slice_in_dim(cotangent, start_row, half_rows, 0).astype(jnp.float32)
    grad_frames = (
        my_cotangent + norm_back(feature_grads, my_unit, my_inverse) + mean_grads
    ).astype(jnp.bfloat16)
    glob_cols = glob_normed.astype(jnp.float32)
    inner = lax.dot_general(
        normed, grad_cat, (((0,), (0,)), ((), ())), preferred_element_type=jnp.float32
    )
    glob_term = lax.dot_general(glob_cols, glob_grads, (((0,), (0,)), ((), ())), precision=PRECISE)
    inner = inner + jnp.concatenate(
        [
            jnp.zeros((width // shard_total * lax.axis_size("tm"), local_width), jnp.float32),
            glob_term,
        ],
        1,
    )
    last_term = lax.dot_general(
        cotangent, attended, (((0,), (0,)), ((), ())), preferred_element_type=jnp.float32
    )
    grad_weights = lax.psum_scatter(
        jnp.concatenate(
            [
                inner.reshape(width // shard_total * lax.axis_size("tm"), 3, local_width),
                last_term.reshape(width // shard_total * lax.axis_size("tm"), 1, local_width),
            ],
            1,
        ),
        "tm",
        scatter_dimension=0,
        tiled=True,
    )
    return (grad_frames, grad_weights, grad_summary)


def solution(mesh):
    in_specs = (P("tm", None), P("tm", None), P(None, None, "mp"), P(), P())
    out_specs = (P(("tm", "mp"), None), P("tm", None, "mp"), P())
    return jax.shard_map(shards, mesh=mesh, in_specs=in_specs, out_specs=out_specs, check_vma=False)
```

profile of v0, /device:TPU:0, one launch (start us, length us, event | category | flops | bytes accessed | tf_op | source)
XLA Modules:
  0.0 1461.3 jit_solution(6325387271140347531)
XLA Ops:
  7.2 1.6 convert_reduce_fusion
  8.8 7.2 copy.49
  16.0 3.7 convolution_convert_fusion
  19.8 1.1 fusion.36
  20.9 2.1 collective-permute-start
  23.0 4.7 collective-permute-start.1
  27.7 0.6 multiply_reduce_fusion.3
  29.1 0.9 add_multiply_fusion
  30.1 5.9 slice.109
  35.9 3.5 slice.111
  39.4 4.7 copy.50
  44.2 0.8 fusion.26
  44.9 327.5 %all-reduce.14 = bf16[64,1024]{1,0:T(8,128)(2,1)S(1)} all-reduce(f32[64,1024]{1,0:T(8,128)S(1)} %fusion.26), channel_id=1, replica_groups=mesh['tm'=64,'mp'=2] {'tm'}, use_global_device_ids=true, to_apply=%region_5.0 | all-reduce | flops 65536 | bytes 393216 | tf_op jit(solution)/shard_map/psum | solution.py:95
  372.6 0.2 copy.37
  372.8 1.3 fusion.38
  374.1 3.5 convolution_convert_fusion.2
  377.7 0.4 fusion.7
  378.2 251.0 %all-reduce.9.cloned.1.call-done = f32[64,1024]{1,0:T(8,128)} async-done(((f32[64,1024]{1,0:T(8,128)}), f32[64,1024]{1,0:T(8,128)}) %all-reduce.9.cloned.1.call-update) | async-done | bytes 262160 | tf_op jit(solution)/shard_map/psum | solution.py:95
  629.1 1.1 multiply_reduce_fusion
  630.2 2.3 pad_maximum_fusion.2
  632.5 2.2 copy.36
  634.7 4.6 fusion.3
  639.4 4.4 fusion.4
  643.7 1.5 copy-done.1
  645.5 2.3 pad_maximum_fusion.3
  647.7 2.3 copy.41
  650.0 15.3 %fusion = (f32[8,512]{1,0:T(8,128)S(1)}, bf16[8,512,1024]{2,1,0:T(8,128)(2,1)}, f32[8,512,1024]{2,1,0:T(8,128)}) fusion(f32[8,512]{1,0:T(8,128)S(1)} %add.160, f32[8,512]{1,0:T(8,128)S(1)} %max.8, f32[8,512,1024]{2,1,0:T(8,128)} %copy-done.1, pred[512,1024]{1,0:T(8,128)(4,1)S(1)} %fusion.7, bf16[512,8,64]{0,2,1:T(8,128)(2,1)} %bitcast.95, ...), kind=kOutput, calls=%fused_computation.2 | convolution fusion | flops 570421248 | bytes 44089344 | tf_op jit(solution)/shard_map/qhe,khe->hqk/dot_general | solution.py:30
  665.4 0.4 fusion.10
  665.8 0.2 fusion.12
  666.0 1.3 fusion.39
  667.3 1.0 fusion.40
  668.2 1.0 fusion.41
  669.2 0.3 fusion.42
  669.5 1.6 convolution_bitcast_fusion
  671.1 8.3 fusion.2
  679.4 1.6 convolution_bitcast_fusion.1
  681.0 5.5 fusion.8
  686.5 1.3 collective-permute-start.2
  687.9 1.4 collective-permute-start.3
  689.4 2.7 fusion.9
  692.1 2.0 fusion.25
  694.0 0.8 pad_maximum_fusion.6
  694.9 0.6 copy-done.13
  695.5 2.1 convolution_bitcast_fusion.2
  697.9 0.6 copy-done.17
  698.5 0.2 copy-done.18
  698.7 4.7 pad_add_fusion
  703.4 6.6 copy.45
  710.1 8.3 pad_maximum_fusion
  718.4 10.2 copy.47
  728.7 5.2 convolution_convert_fusion.1
  733.9 659.6 %all-reduce.11.cloned.1.call-done = (f32[64,1024]{0,1:T(8,128)}, f32[1024,4,512]{2,1,0:T(4,128)}) async-done(((f32[64,1024]{0,1:T(8,128)}, f32[1024,4,512]{2,1,0:T(4,128)}), (f32[64,1024]{0,1:T(8,128)}, f32[1024,4,512]{2,1,0:T(4,128)})) %all-reduce.11.cloned.1.call-update) | async-done | bytes 8650768 | tf_op jit(solution)/shard_map/psum | solution.py:158
  1393.5 3.0 convolution_convert_fusion.3
  1396.6 0.6 dynamic-slice.24
  1397.8 0.2 convert_multiply_fusion.2
  1398.0 1.7 constant_dynamic-slice_fusion
  1399.7 47.3 %all-reduce.13.cloned.1.call-done = (bf16[64,1024]{1,0:T(8,128)(2,1)}, bf16[512,1024]{1,0:T(8,128)(2,1)}) async-done(((bf16[64,1024]{1,0:T(8,128)(2,1)}, bf16[512,1024]{1,0:T(8,128)(2,1)}), (bf16[64,1024]{1,0:T(8,128)(2,1)}, bf16[512,1024]{1,0:T(8,128)(2,1)})) %all-reduce.13.cloned.1.call-update) | async-done | bytes 1179664 | tf_op jit(solution)/shard_map/psum | solution.py:162
  1447.0 1.2 fusion.17
  1448.2 1.1 fusion.23
  1449.3 1.0 fusion.24
  1450.4 0.7 copy-done.20
  1451.1 0.2 fusion.30
  1451.3 0.6 multiply_reduce_fusion.2
  1452.6 2.2 fusion.16
  (79 shorter events, 1.4 us)
Async XLA Ops:
  7.2 622.0 %all-reduce.9.cloned.1.call-start = ((), (), s32[]{:S(2)}) async-start(), calls=%async_computation | async-start | bytes 524288 | tf_op jit(solution)/shard_map/psum | solution.py:95
  8.8 7.2 copy-start.3
  19.8 9.3 copy-start.22
  19.8 9.3 copy-start.21
  20.9 609.3 %collective-permute-start = (bf16[512,512]{1,0:T(8,128)(2,1)}, bf16[512,512]{1,0:T(8,128)(2,1)}, u32[]{:S(2)}, u32[]{:S(2)}) collective-permute-start(bf16[512,512]{1,0:T(8,128)(2,1)} %get-tuple-element.98), channel_id=1, source_target_pairs={{0,2},{2,4},{4,6},{6,8},{8,10},{10,12},{12,14},{14,16},{16,18},{18... | collective-permute-start | bytes 1572872 | tf_op jit(solution)/shard_map/ppermute | solution.py:17
  23.0 622.4 %collective-permute-start.1 = (bf16[512,512]{1,0:T(8,128)(2,1)}, bf16[512,512]{1,0:T(8,128)(2,1)}, u32[]{:S(2)}, u32[]{:S(2)}) collective-permute-start(bf16[512,512]{1,0:T(8,128)(2,1)} %get-tuple-element.96), channel_id=1, source_target_pairs={{0,2},{2,4},{4,6},{6,8},{8,10},{10,12},{12,14},{14,16},{16,18},{18... | collective-permute-start | bytes 1572872 | tf_op jit(solution)/shard_map/ppermute | solution.py:17
  30.0 1363.5 %all-reduce.11.cloned.1.call-start = ((), (), s32[]{:S(2)}) async-start(), calls=%async_computation.1 | async-start | bytes 17825792 | tf_op jit(solution)/shard_map/psum | solution.py:158
  30.1 5.9 copy-start.2
  639.3 5.9 copy-start.1
  639.3 5.9 copy-start.9
  650.0 15.3 %copy-start.10 = (f32[8,512,64]{1,2,0:T(8,128)S(1)}, f32[8,512,64]{1,2,0:T(8,128)}, u32[]{:S(2)}) copy-start(f32[8,512,64]{1,2,0:T(8,128)} %get-tuple-element.106) | copy-start | bytes 3145732
  650.0 15.3 %copy-start.12 = (bf16[512,512]{0,1:T(8,128)(2,1)S(1)}, bf16[512,512]{0,1:T(8,128)(2,1)}, u32[]{:S(2)}) copy-start(bf16[512,512]{0,1:T(8,128)(2,1)} %convolution_convert_fusion.2) | copy-start | bytes 1572868
  665.3 4.1 copy-start
  671.1 23.8 %copy-start.6 = (f32[1024,8,64]{0,2,1:T(8,128)}, f32[1024,8,64]{0,2,1:T(8,128)S(1)}, u32[]{:S(2)}) copy-start(f32[1024,8,64]{0,2,1:T(8,128)S(1)} %convolution_bitcast_fusion) | copy-start | bytes 6291460
  679.4 1.6 copy-start.5
  681.0 13.9 copy-start.7
  681.0 8.4 copy-start.11
  686.5 11.0 collective-permute-start.2
  687.9 4.1 copy-start.8
  687.9 4.1 copy-start.15
  687.9 4.1 copy-start.16
  687.9 9.8 collective-permute-start.3
  694.0 1.4 copy-start.13
  694.9 2.7 slice-start.1
  694.9 2.9 slice-start
  695.4 3.3 copy-start.4
  695.5 3.3 copy-start.19
  697.7 0.8 copy-start.17
  697.9 0.8 copy-start.18
  728.7 718.3 %all-reduce.13.cloned.1.call-start = ((), (), s32[]{:S(2)}) async-start(), calls=%async_computation.2 | async-start | bytes 2359296 | tf_op jit(solution)/shard_map/psum | solution.py:162
  733.9 662.7 %copy-start.23 = (u32[128]{0:T(128)S(1)}, u32[128]{0:T(128)}, u32[]{:S(2)}) copy-start(u32[128]{0:T(128)} %constant.186) | copy-start | bytes 1540
  1398.0 54.5 %copy-start.14 = (bf16[512,1024]{1,0:T(8,128)(2,1)S(1)}, bf16[512,1024]{1,0:T(8,128)(2,1)}, u32[]{:S(2)}) copy-start(bf16[512,1024]{1,0:T(8,128)(2,1)} %param.22) | copy-start | bytes 3145732
  1450.4 0.7 copy-start.20
Sparse Core Ops, SparseCore 0:
  30.1 598.9 all-reduce.8
  728.8 664.6 all-reduce.10
  1396.6 50.3 all-reduce.12
where the time goes:
time: 1460 us
  waiting for transfers between devices  958 us (66%)
  blocking collectives  327 us (22%)
  matrix products  61.5 us (4%)
  local copies, waits for them, and re-layouts  50.5 us (3%)
  other arithmetic  38 us (3%)
  between operations  16.3 us (1%)
    psum x1, waiting for transfers between devices, shards(): glob_total = lax.psum(glob_grads, 'tm')  660 us
    psum x1, blocking collectives, shards(): anchor, glob_kv32 = lax.psum((anchor_own, kv_own), 'tm')  327 us
    psum x1, waiting for transfers between devices, shards(): anchor, glob_kv32 = lax.psum((anchor_own, kv_own), 'tm')  251 us
    psum x1, waiting for transfers between devices, shards(): lax.psum(local_features.astype(jnp.bfloat16), 'mp').astype(jnp.float32)  47.3 us
    dot_general x12, matrix products, product(): return jnp.einsum(form, left, right, preferred_element_type=jnp.float32)  36.4 us
  transfers between devices with their start and end apart: 7, of which 3 were waited for; matrix products, arithmetic and copies ran while one was open for 4% of the time, Pallas kernels for 0%

commit v1 on v0

--- a/solution.py
+++ b/solution.py
@@ -81,21 +81,22 @@
     glob_count = summary.shape[0]
     shard_index = lax.axis_index("tm")
     shard_total = lax.axis_size("tm")
+    mp_index = lax.axis_index("mp")
+    mp_total = lax.axis_size("mp")
     frames32 = frames.astype(jnp.float32)
     unit_rows, inverse = normalize(frames32)
     normed = unit_rows.astype(jnp.bfloat16)
     block_mean = jnp.mean(frames32, axis=0, keepdims=True)
     pool_unit, pool_inv = normalize(block_mean)
     pooled = pool_unit.astype(jnp.bfloat16)
+    pooled_rows = jnp.concatenate([pooled, frames[1:8]], 0)
+    pooled_all = lax.all_gather(pooled_rows, "tm", axis=0, tiled=False)[:, 0, :]
     owned_mask = (owners == shard_index).astype(jnp.float32)[:, None]
+    anchor = summary.astype(jnp.float32) + jnp.take(pooled_all, owners, axis=0).astype(jnp.float32)
+    glob_unit, glob_inv = normalize(anchor)
+    glob_normed = glob_unit.astype(jnp.bfloat16)
     kv_weights = weights[:, 1:3, :].reshape(width, 2 * local_width)
-    anchor_own = (summary.astype(jnp.float32) + pooled.astype(jnp.float32)) * owned_mask
-    own_unit, own_inv = normalize(anchor_own)
-    kv_own = jnp.dot(own_unit.astype(jnp.bfloat16), kv_weights, preferred_element_type=jnp.float32)
-    anchor, glob_kv32 = lax.psum((anchor_own, kv_own), "tm")
-    glob_unit, glob_inv = normalize(anchor)
-    glob_kv = glob_kv32.astype(jnp.bfloat16)
-    glob_normed = glob_unit.astype(jnp.bfloat16)
+    glob_kv = jnp.dot(glob_normed, kv_weights, preferred_element_type=jnp.float32).astype(jnp.bfloat16)
     project = weights[:, :3, :].reshape(width, 3 * local_width)
     qkv = jnp.dot(normed, project, preferred_element_type=jnp.float32).astype(jnp.bfloat16)
     keys_local = qkv[:, local_width : 2 * local_width]
@@ -114,64 +115,45 @@
     )
     keys_glob = glob_kv[:, :local_width].reshape(glob_count, heads_here, HEAD_DIM)
     values_glob = glob_kv[:, local_width:].reshape(glob_count, heads_here, HEAD_DIM)
-    grad_kp = jnp.zeros((rows_here + WINDOW, heads_here, HEAD_DIM), jnp.float32)
-    grad_vp = jnp.zeros((rows_here + WINDOW, heads_here, HEAD_DIM), jnp.float32)
     allowed = window_mask(WINDOW, WINDOW, shard_index * rows_here + 0)
     results = block_pass(
         queries, keys_ext, values_ext, keys_glob, values_glob, grad_attended, allowed
     )
-    attended_parts = results[0]
-    query_parts = results[1]
-    grad_kp = grad_kp.at[0 : 2 * WINDOW].add(results[2])
-    grad_vp = grad_vp.at[0 : 2 * WINDOW].add(results[3])
-    grad_kg = results[4]
-    grad_vg = results[5]
-    attended = attended_parts.reshape(rows_here, local_width)
-    grad_queries = query_parts.reshape(rows_here, local_width)
-    back_keys, back_values = (
-        from_behind(
-            grad_kp[:WINDOW].reshape(WINDOW, local_width).astype(jnp.bfloat16), "tm", -1
-        ).astype(jnp.float32),
-        from_behind(
-            grad_vp[:WINDOW].reshape(WINDOW, local_width).astype(jnp.bfloat16), "tm", -1
-        ).astype(jnp.float32),
+    attended = results[0].reshape(rows_here, local_width)
+    grad_queries = results[1].reshape(rows_here, local_width)
+    grad_kp = results[2].reshape(rows_here + WINDOW, local_width)
+    grad_vp = results[3].reshape(rows_here + WINDOW, local_width)
+    grad_kg = results[4].reshape(glob_count, local_width)
+    grad_vg = results[5].reshape(glob_count, local_width)
+    back_keys, back_values = from_behind(
+        (grad_kp[:WINDOW].astype(jnp.bfloat16), grad_vp[:WINDOW].astype(jnp.bfloat16)), "tm", -1
     )
-    grad_keys = (
-        grad_kp[WINDOW:]
-        .reshape(rows_here, local_width)
-        .at[rows_here - WINDOW :]
-        .add(back_keys)
-        .astype(jnp.bfloat16)
+    grad_keys = grad_kp[WINDOW:].at[rows_here - WINDOW :].add(back_keys.astype(jnp.float32))
+    grad_values = grad_vp[WINDOW:].at[rows_here - WINDOW :].add(back_values.astype(jnp.float32))
+    grad_cat = jnp.concatenate(
+        [grad_queries, grad_keys.astype(jnp.bfloat16), grad_values.astype(jnp.bfloat16)], 1
     )
-    grad_values = (
-        grad_vp[WINDOW:]
-        .reshape(rows_here, local_width)
-        .at[rows_here - WINDOW :]
-        .add(back_values)
-        .astype(jnp.bfloat16)
+    glob_grads = jnp.concatenate([grad_kg, grad_vg], 1)
+    kv_weights32 = kv_weights.astype(jnp.float32)
+    local_features = lax.dot_general(
+        glob_grads, kv_weights32, (((1,), (1,)), ((), ())), precision=PRECISE
     )
-    grad_cat = jnp.concatenate([grad_queries, grad_keys, grad_values], 1)
-    glob_grads = jnp.concatenate(
-        [grad_kg.reshape(glob_count, local_width), grad_vg.reshape(glob_count, local_width)], 1
-    )
-    kv_weights32 = kv_weights.astype(jnp.float32)
-    glob_total = lax.psum(glob_grads, "tm")
-    local_features = lax.dot_general(
-        glob_total, kv_weights32, (((1,), (1,)), ((), ())), precision=PRECISE
-    )
-    summary_features = lax.psum(local_features.astype(jnp.bfloat16), "mp").astype(jnp.float32)
+    summary_features = lax.psum(local_features, ("tm", "mp"))
     grad_summary = norm_back(summary_features, glob_unit, glob_inv)
     pool_grads = lax.dot_general(
         owned_mask, grad_summary, (((0,), (0,)), ((), ())), precision=PRECISE
     )
     mean_grads = norm_back(pool_grads, pool_unit, pool_inv) / rows_here
-    half_rows = rows_here // lax.axis_size("mp")
-    start_row = lax.axis_index("mp") * half_rows
+    half_rows = rows_here // mp_total
+    start_row = mp_index * half_rows
+    other_row = (1 - mp_index) * half_rows
     feature_all = lax.dot_general(
         grad_cat, project, (((1,), (1,)), ((), ())), preferred_element_type=jnp.float32
     )
-    feature_all = lax.psum(feature_all.astype(jnp.bfloat16), "mp").astype(jnp.float32)
-    feature_grads = lax.dynamic_slice_in_dim(feature_all, start_row, half_rows, 0)
+    mine = lax.dynamic_slice_in_dim(feature_all, start_row, half_rows, 0)
+    theirs = lax.dynamic_slice_in_dim(feature_all, other_row, half_rows, 0).astype(jnp.bfloat16)
+    received = lax.ppermute(theirs, "mp", [(0, 1), (1, 0)])
+    feature_grads = mine + received.astype(jnp.float32)
     my_unit = lax.dynamic_slice_in_dim(unit_rows, start_row, half_rows, 0)
     my_inverse = lax.dynamic_slice_in_dim(inverse, start_row, half_rows, 0)
     my_cotangent = lax.dynamic_slice_in_dim(cotangent, start_row, half_rows, 0).astype(jnp.float32)
@@ -183,28 +165,16 @@
         normed, grad_cat, (((0,), (0,)), ((), ())), preferred_element_type=jnp.float32
     )
     glob_term = lax.dot_general(glob_cols, glob_grads, (((0,), (0,)), ((), ())), precision=PRECISE)
-    inner = inner + jnp.concatenate(
-        [
-            jnp.zeros((width // shard_total * lax.axis_size("tm"), local_width), jnp.float32),
-            glob_term,
-        ],
-        1,
-    )
+    inner = inner + jnp.concatenate([jnp.zeros((width, local_width), jnp.float32), glob_term], 1)
     last_term = lax.dot_general(
         cotangent, attended, (((0,), (0,)), ((), ())), preferred_element_type=jnp.float32
     )
+    weight_parts = jnp.concatenate(
+        [inner.reshape(width, 3, local_width), last_term.reshape(width, 1, local_width)], 1
+    )
     grad_weights = lax.psum_scatter(
-        jnp.concatenate(
-            [
-                inner.reshape(width // shard_total * lax.axis_size("tm"), 3, local_width),
-                last_term.reshape(width // shard_total * lax.axis_size("tm"), 1, local_width),
-            ],
-            1,
-        ),
-        "tm",
-        scatter_dimension=0,
-        tiled=True,
-    )
+        weight_parts.reshape(width, 4 * local_width), "tm", scatter_dimension=0, tiled=True
+    ).reshape(width // shard_total, 4, local_width)
     return (grad_frames, grad_weights, grad_summary)
 
 

time: 1460 us -> 658 us (0.45)
  waiting for transfers between devices: 958 us -> 458 us
  blocking collectives: 327 us -> 0 us
    psum x3 -> x1, waiting for transfers between devices: 958 us -> 108 us  [shards(): summary_features = lax.psum(local_features, ('tm', 'mp'))]
    psum x1 -> x0, blocking collectives: 327 us -> none  [shards(): anchor, glob_kv32 = lax.psum((anchor_own, kv_own), 'tm')]
    unnamed x3 -> x4, waiting for transfers between devices: 0.06 us -> 320 us
    all_gather x0 -> x1, waiting for transfers between devices: none -> 15.4 us  [shards(): pooled_all = lax.all_gather(pooled_rows, 'tm', axis=0, tiled=False)[:, 0, :]]
  transfers between devices with their start and end apart: 7 -> 8, of which waited for: 3 -> 4; matrix products, arithmetic and copies ran while one was open for 4% -> 16% of each run, Pallas kernels for 0% -> 0%
where the time goes in v1:
time: 658 us; the launch traced here: 657 us
  waiting for transfers between devices  458 us (70%)
  matrix products  74.9 us (11%)
  local copies, waits for them, and re-layouts  53.8 us (8%)
  other arithmetic  44.4 us (7%)
  between operations  15.7 us (2%)
  starting transfers between devices  10.3 us (2%)
    unnamed x4, waiting for transfers between devices  320 us
    psum x1, waiting for transfers between devices, shards(): summary_features = lax.psum(local_features, ('tm', 'mp'))  108 us
    dot_general x12, matrix products, product(): return jnp.einsum(form, left, right, preferred_element_type=jnp.float32)  48.1 us
    unnamed x82, local copies, waits for them, and re-layouts  26 us
    all_gather x1, waiting for transfers between devices, shards(): pooled_all = lax.all_gather(pooled_rows, 'tm', axis=0, tiled=False)[:, 0, :]  15.4 us
    ppermute x1, waiting for transfers between devices, shards(): received = lax.ppermute(theirs, 'mp', [(0, 1), (1, 0)])  13.8 us
  transfers between devices with their start and end apart: 8, of which 4 were waited for; matrix products, arithmetic and copies ran while one was open for 16% of the time, Pallas kernels for 0%

profile of v1, /device:TPU:0, one launch (start us, length us, event | category | flops | bytes accessed | tf_op | source)
XLA Modules:
  0.0 656.9 jit_solution(17877938529414240924)
XLA Ops:
  7.2 1.6 convert_reduce_fusion
  8.8 0.7 slice.83
  11.6 7.3 %copy.53 = bf16[1024,3,512]{0,2,1:T(8,128)(2,1)} copy(bf16[1024,3,512]{2,1,0:T(4,128)(2,1)} %bitcast.92) | data formatting | bytes 6291456
  18.8 3.9 convolution_convert_fusion
  22.7 1.1 fusion.33
  23.9 2.1 collective-permute-start
  26.0 4.7 collective-permute-start.1
  30.6 3.5 slice.85
  34.1 3.5 slice.87
  37.6 4.7 copy.55
  43.1 3.5 convolution_convert_fusion.1
  46.6 2.3 pad_maximum_fusion.2
  48.8 2.3 copy.37
  51.1 2.3 pad_maximum_fusion.3
  53.4 2.3 copy.43
  55.7 9.2 %fusion.3 = (f32[8,512]{1,0:T(8,128)}, f32[8,512,1024]{2,1,0:T(8,128)}) fusion(pred[512,1024]{1,0:T(8,128)(4,1)S(1)} %fusion.7, bf16[512,8,64]{0,2,1:T(8,128)(2,1)S(1)} %bitcast.93, bf16[1024,8,64]{0,2,1:T(8,128)(2,1)} %bitcast.98), kind=kOutput, calls=%fused_computation.9 | convolution fusion | flops 549449728 | bytes 18890752 | tf_op jit(solution)/shard_map/qhe,khe->hqk/dot_general | solution.py:30
  64.9 15.4 %all-gather.3.cloned.1.call-done = bf16[512,1024]{1,0:T(8,128)(2,1)} async-done(((bf16[8,1024]{1,0:T(8,128)(2,1)}), bf16[512,1024]{1,0:T(8,128)(2,1)}) %all-gather.3.cloned.1.call-update) | async-done | bytes 1048592 | tf_op jit(solution)/shard_map/all_gather | solution.py:93
  80.3 1.4 slice.100
  81.7 0.7 gather_fusion
  82.7 0.8 convolution_convert_fusion.2
  84.1 1.0 copy.57
  85.5 0.7 max.8
  86.5 0.8 fusion.15
  87.2 8.6 %fusion.4 = f32[8,512]{1,0:T(8,128)} fusion(f32[8,512,1024]{2,1,0:T(8,128)} %get-tuple-element.58, f32[8,512]{1,0:T(8,128)S(1)} %max.8, pred[512,1024]{1,0:T(8,128)(4,1)S(1)} %fusion.7), kind=kLoop, calls=%fused_computation.10 | loop fusion | flops 16773120 | bytes 17334272 | tf_op jit(solution)/shard_map/reduce_sum | solution.py:50
  95.8 1.0 copy.58
  96.8 0.9 add.144
  97.7 1.8 fusion.10
  99.5 16.4 %fusion = (f32[8,512]{1,0:T(8,128)S(1)}, bf16[8,512,1024]{2,1,0:T(8,128)(2,1)}, f32[8,512,1024]{2,1,0:T(8,128)}) fusion(f32[8,512]{1,0:T(8,128)S(1)} %add.144, f32[8,512]{1,0:T(8,128)S(1)} %max.8, f32[8,512,1024]{2,1,0:T(8,128)} %get-tuple-element.58, pred[512,1024]{1,0:T(8,128)(4,1)S(1)} %fusion.7, bf16[512,8,64]{0,2,1:T(8,128)(2,1)S(1)} %bitcast.106, ...), kind=kOutput, calls=%fused_computation.3 | convolution fusion | flops 570421248 | bytes 44089344 | tf_op jit(solution)/shard_map/qhe,khe->hqk/dot_general | solution.py:30
  115.9 1.0 fusion.38
  117.1 1.0 fusion.37
  118.1 1.3 fusion.36
  119.4 1.3 fusion.39
  120.6 5.3 convolution_bitcast_fusion
  126.0 8.2 %fusion.2 = bf16[8,512,1024]{2,1,0:T(8,128)(2,1)S(1)} fusion(bf16[8,512,1024]{2,1,0:T(8,128)(2,1)S(1)} %bitcast.87, f32[8,512,1024]{2,1,0:T(8,128)} %get-tuple-element.61, f32[8,512]{1,0:T(8,128)S(1)} %add.145), kind=kLoop, calls=%fused_computation.5 | loop fusion | flops 20971520 | bytes 33570816 | tf_op jit(solution)/shard_map/convert_element_type | solution.py:64
  134.3 1.6 convolution_bitcast_fusion.1
  135.9 5.5 fusion.8
  141.3 0.9 slice.111
  142.2 1.3 collective-permute-start.2
  143.5 0.9 slice.110
  144.4 1.4 collective-permute-start.3
  145.8 3.5 fusion.9
  149.3 3.9 fusion.19
  153.2 2.0 fusion.20
  155.3 3.6 convolution_bitcast_fusion.2
  158.9 1.2 fusion.14
  160.2 1.3 fusion.13
  161.5 0.8 copy-done.19
  162.3 4.7 pad_add_fusion
  167.0 6.8 %copy.47 = f32[1024,1536]{0,1:T(8,128)} copy(f32[1024,1536]{1,0:T(8,128)} %pad_add_fusion) | data formatting | bytes 12582912 | tf_op jit(solution)/shard_map/add | solution.py:168
  173.8 7.5 %pad_maximum_fusion = f32[1024,4,512]{0,2,1:T(8,128)} fusion(f32[1024,1,512]{0,2,1:T(8,128)S(1)} %copy-done.7, f32[1024,3,512]{0,2,1:T(8,128)} %bitcast.89), kind=kLoop, calls=%fused_computation.11 | loop fusion | flops 2097152 | bytes 16777216 | tf_op jit(solution)/shard_map/concatenate | solution.py:172
  181.3 9.2 %copy.51 = f32[1024,2048]{1,0:T(8,128)} copy(f32[1024,2048]{0,1:T(8,128)} %bitcast.88) | data formatting | bytes 16777216
  190.8 108.3 %all-reduce.3.cloned.1.call-done = f32[64,1024]{1,0:T(8,128)} async-done(((f32[64,1024]{1,0:T(8,128)}), f32[64,1024]{1,0:T(8,128)}) %all-reduce.3.cloned.1.call-update) | async-done | bytes 262160 | tf_op jit(solution)/shard_map/psum | solution.py:141
  299.1 1.2 multiply_reduce_fusion.1
  300.3 1.1 subtract_multiply_fusion
  301.4 4.3 fusion.16
  305.7 1.4 copy-done.12
  307.1 0.9 dynamic-slice_convert_fusion
  308.0 0.7 collective-permute-start.4
  310.2 13.8 %collective-permute-done.4 = bf16[256,1024]{1,0:T(8,128)(2,1)} collective-permute-done((bf16[256,1024]{1,0:T(8,128)(2,1)}, bf16[256,1024]{1,0:T(8,128)(2,1)}, u32[]{:S(2)}, u32[]{:S(2)}) %collective-permute-start.4) | collective-permute-done | bytes 524320 | tf_op jit(solution)/shard_map/ppermute | solution.py:155
  324.0 1.6 multiply_reduce_fusion
  325.6 2.2 add_convert_fusion
  327.9 320.3 %reduce-scatter.4.cloned.1.call-done = f32[16,2048]{1,0:T(8,128)} async-done(((f32[1024,2048]{1,0:T(8,128)}), f32[16,2048]{1,0:T(8,128)}) %reduce-scatter.4.cloned.1.call-update) | async-done | bytes 131088
  648.2 1.2 copy.52
  649.4 1.0 copy.49
  (115 shorter events, 5.1 us)
Async XLA Ops:
  7.2 73.1 %all-gather.3.cloned.1.call-start = ((), (), s32[]{:S(2)}) async-start(), calls=%async_computation.2 | async-start | bytes 1064960 | tf_op jit(solution)/shard_map/all_gather | solution.py:93
  8.8 2.8 copy-start.26
  11.5 287.6 %all-reduce.3.cloned.1.call-start = ((), (), s32[]{:S(2)}) async-start(), calls=%async_computation.1 | async-start | bytes 524288 | tf_op jit(solution)/shard_map/psum | solution.py:141
  11.6 7.3 %copy-start.28 = (f32[512]{0:T(512)}, f32[512]{0:T(512)S(1)}, u32[]{:S(2)}) copy-start(f32[512]{0:T(512)S(1)} %add_rsqrt_fusion) | copy-start | bytes 6148
  11.6 7.3 %copy-start.2 = (bf16[512,1024]{1,0:T(8,128)(2,1)S(1)}, bf16[512,1024]{1,0:T(8,128)(2,1)}, u32[]{:S(2)}) copy-start(bf16[512,1024]{1,0:T(8,128)(2,1)} %param.13) | copy-start | bytes 3145732
  18.8 11.8 %copy-start = (bf16[1024,4,512]{2,1,0:T(4,128)(2,1)S(1)}, bf16[1024,4,512]{2,1,0:T(4,128)(2,1)}, u32[]{:S(2)}) copy-start(bf16[1024,4,512]{2,1,0:T(4,128)(2,1)} %param.15) | copy-start | bytes 12582916
  23.9 22.7 %collective-permute-start = (bf16[512,512]{1,0:T(8,128)(2,1)}, bf16[512,512]{1,0:T(8,128)(2,1)}, u32[]{:S(2)}, u32[]{:S(2)}) collective-permute-start(bf16[512,512]{1,0:T(8,128)(2,1)} %get-tuple-element.52), channel_id=1, source_target_pairs={{0,2},{2,4},{4,6},{6,8},{8,10},{10,12},{12,14},{14,16},{16,18},{18... | collective-permute-start | bytes 1572872 | tf_op jit(solution)/shard_map/ppermute | solution.py:17
  26.0 25.2 %collective-permute-start.1 = (bf16[512,512]{1,0:T(8,128)(2,1)}, bf16[512,512]{1,0:T(8,128)(2,1)}, u32[]{:S(2)}, u32[]{:S(2)}) collective-permute-start(bf16[512,512]{1,0:T(8,128)(2,1)} %get-tuple-element.53), channel_id=1, source_target_pairs={{0,2},{2,4},{4,6},{6,8},{8,10},{10,12},{12,14},{14,16},{16,18},{18... | collective-permute-start | bytes 1572872 | tf_op jit(solution)/shard_map/ppermute | solution.py:17
  37.6 5.0 copy-start.34
  43.1 39.6 %copy-start.30 = (pred[64]{0:T(512)(128)(4,1)}, pred[64]{0:T(512)(128)(4,1)S(1)}, u32[]{:S(2)}) copy-start(pred[64]{0:T(512)(128)(4,1)S(1)} %compare_and_fusion) | copy-start | bytes 196
  55.7 26.8 %copy-start.11 = (bf16[64,1024]{1,0:T(8,128)(2,1)S(1)}, bf16[64,1024]{1,0:T(8,128)(2,1)}, u32[]{:S(2)}) copy-start(bf16[64,1024]{1,0:T(8,128)(2,1)} %param.16) | copy-start | bytes 393220
  82.7 1.5 copy-start.32
  85.1 10.7 %copy-start.21 = (bf16[64,512]{0,1:T(8,128)(2,1)}, bf16[64,512]{0,1:T(8,128)(2,1)S(1)}, u32[]{:S(2)}) copy-start(bf16[64,512]{0,1:T(8,128)(2,1)S(1)} %copy.57) | copy-start | bytes 196612
  85.5 1.0 copy-start.8
  96.8 19.1 %copy-start.24 = (bf16[64,512]{0,1:T(8,128)(2,1)}, bf16[64,512]{0,1:T(8,128)(2,1)S(1)}, u32[]{:S(2)}) copy-start(bf16[64,512]{0,1:T(8,128)(2,1)S(1)} %copy.58) | copy-start | bytes 196612
  96.8 2.7 copy-start.9
  96.8 2.7 copy-start.14
  115.9 2.2 copy-start.22
  115.9 3.4 copy-start.25
  119.4 6.6 %slice-start = ((s8[8388608]{0:T(1024)(128)(4,1)}), s8[4194304]{0:T(1024)(128)(4,1)S(1)}, s32[]{:S(2)}) async-start(s8[8388608]{0:T(1024)(128)(4,1)} %bitcast.86), calls=%async_computation.4 | async-start | bytes 8388608
  120.6 5.3 slice-start.1
  126.0 17.5 %copy-start.5 = (f32[1024,8,64]{0,2,1:T(8,128)}, f32[1024,8,64]{0,2,1:T(8,128)S(1)}, u32[]{:S(2)}) copy-start(f32[1024,8,64]{0,2,1:T(8,128)S(1)} %convolution_bitcast_fusion) | copy-start | bytes 6291460
  134.2 1.6 copy-start.4
  135.8 5.5 copy-start.6
  135.8 10.0 %copy-start.10 = (f32[8,64,512]{2,1,0:T(8,128)S(1)}, f32[8,64,512]{2,1,0:T(8,128)}, u32[]{:S(2)}) copy-start(f32[8,64,512]{2,1,0:T(8,128)} %fusion.39) | copy-start | bytes 3145732
  142.2 16.7 %collective-permute-start.2 = (bf16[512,512]{0,1:T(8,128)(2,1)}, bf16[512,512]{0,1:T(8,128)(2,1)}, u32[]{:S(2)}, u32[]{:S(2)}) collective-permute-start(bf16[512,512]{0,1:T(8,128)(2,1)} %bitcast.13), channel_id=1, source_target_pairs={{2,0},{4,2},{6,4},{8,6},{10,8},{12,10},{14,12},{16,14},{18,16},{20... | collective-permute-start | bytes 1572872 | tf_op jit(solution)/shard_map/ppermute | solution.py:17
  144.4 4.9 copy-start.16
  144.4 4.9 copy-start.17
  144.4 4.9 copy-start.31
  144.4 4.9 copy-start.33
  144.4 15.8 %collective-permute-start.3 = (bf16[512,512]{0,1:T(8,128)(2,1)}, bf16[512,512]{0,1:T(8,128)(2,1)}, u32[]{:S(2)}, u32[]{:S(2)}) collective-permute-start(bf16[512,512]{0,1:T(8,128)(2,1)} %bitcast.16), channel_id=1, source_target_pairs={{2,0},{4,2},{6,4},{8,6},{10,8},{12,10},{14,12},{16,14},{18,16},{20... | collective-permute-start | bytes 1572872 | tf_op jit(solution)/shard_map/ppermute | solution.py:17
  155.2 3.7 slice-start.3
  155.2 5.0 slice-start.2
  155.2 493.0 %reduce-scatter.4.cloned.1.call-start = ((), (), s32[]{:S(2)}) async-start(), calls=%async_computation.3 | async-start | bytes 8519680
  155.3 7.1 %copy-start.1 = (f32[1024,1024]{1,0:T(8,128)S(1)}, f32[1024,1024]{1,0:T(8,128)}, u32[]{:S(2)}) copy-start(f32[1024,1024]{1,0:T(8,128)} %fusion.19) | copy-start | bytes 12582916
  155.3 7.0 %copy-start.3 = (bf16[512,1024]{1,0:T(8,128)(2,1)S(1)}, bf16[512,1024]{1,0:T(8,128)(2,1)}, u32[]{:S(2)}) copy-start(bf16[512,1024]{1,0:T(8,128)(2,1)} %param.13) | copy-start | bytes 3145732
  155.3 7.0 %copy-start.20 = (bf16[8,64,512]{2,1,0:T(8,128)(2,1)S(1)}, bf16[8,64,512]{2,1,0:T(8,128)(2,1)}, u32[]{:S(2)}) copy-start(bf16[8,64,512]{2,1,0:T(8,128)(2,1)} %fusion.8) | copy-start | bytes 1572868
  155.3 7.0 %copy-start.29 = (f32[512]{0:T(512)S(1)}, f32[512]{0:T(512)}, u32[]{:S(2)}) copy-start(f32[512]{0:T(512)} %copy-done.28) | copy-start | bytes 6148
  160.1 1.4 copy-start.18
  161.5 0.8 copy-start.19
  167.0 6.8 %copy-start.7 = (f32[1024,1,512]{0,2,1:T(8,128)S(1)}, f32[1024,1,512]{0,2,1:T(8,128)}, u32[]{:S(2)}) copy-start(f32[1024,1,512]{0,2,1:T(8,128)} %convolution_bitcast_fusion.2) | copy-start | bytes 6291460
  301.4 7.3 %copy-start.23 = (f32[64,1024]{1,0:T(8,128)}, f32[64,1024]{1,0:T(8,128)S(1)}, u32[]{:S(2)}) copy-start(f32[64,1024]{1,0:T(8,128)S(1)} %subtract_multiply_fusion) | copy-start | bytes 786436
  301.4 7.3 %copy-start.35 = (s32[64]{0:T(128)S(1)}, s32[64]{0:T(128)}, u32[]{:S(2)}) copy-start(s32[64]{0:T(128)} %param.17) | copy-start | bytes 772
  301.4 7.5 %copy-start.27 = (f32[1024]{0:T(1024)S(1)}, f32[1024]{0:T(1024)}, u32[]{:S(2)}) copy-start(f32[1024]{0:T(1024)} %copy-done.26) | copy-start | bytes 12292
  305.7 1.4 copy-start.12
  307.1 18.5 %copy-start.15 = (bf16[512,1024]{1,0:T(8,128)(2,1)S(1)}, bf16[512,1024]{1,0:T(8,128)(2,1)}, u32[]{:S(2)}) copy-start(bf16[512,1024]{1,0:T(8,128)(2,1)} %param.14) | copy-start | bytes 3145732
  308.0 16.0 %collective-permute-start.4 = (bf16[256,1024]{1,0:T(8,128)(2,1)}, bf16[256,1024]{1,0:T(8,128)(2,1)}, u32[]{:S(2)}, u32[]{:S(2)}) collective-permute-start(bf16[256,1024]{1,0:T(8,128)(2,1)} %dynamic-slice_convert_fusion), channel_id=1, source_target_pairs={{0,1},{1,0},{2,3},{3,2},{4,5},{5,4},{6,7},{7,6},{8,9},{9,8},{10,11... | collective-permute-start | bytes 1572872 | tf_op jit(solution)/shard_map/ppermute | solution.py:155
  310.1 15.5 %copy-start.13 = (f32[512,1024]{1,0:T(8,128)S(1)}, f32[512,1024]{1,0:T(8,128)}, u32[]{:S(2)}) copy-start(f32[512,1024]{1,0:T(8,128)} %copy-done.12) | copy-start | bytes 6291460
Sparse Core Ops, SparseCore 0:
  11.8 68.4 all-gather.2
  155.3 143.7 all-reduce.2
  301.5 346.6 reduce-scatter.3
